TPU v7x, 32 devices: a whole 2x2x4 slice. The times are simulated.
32 devices in a mesh: clips: 2 (over y), frame: 4 (over x, core), row: 4 (over z).
Axes of the slice: x: 2, y: 2, z: 4, core: 2. Of those that a mesh axis runs over, the one named last changes fastest.
Arguments:
- frames: bfloat16 [16, 512, 640], P(('clips', 'frame'), 'row'), parts along dimension 0, may hold values from -16 to 16
- key_index: int32 [4], P('clips'), parts along dimension 0, may hold values from 0 to 7, as said below
- w_query: bfloat16 [640, 640], replicated, may hold values from -0.25 to 0.25
- w_keyval: bfloat16 [640, 1280], replicated, may hold values from -0.25 to 0.25
- w_out: bfloat16 [640, 640], replicated, may hold values from -0.25 to 0.25
- norm_gain: float32 [640], replicated, may hold values from 0.1 to 1.9
- w_first: bfloat16 [3, 640, 640], replicated, may hold values from -0.125 to 0.125
- w_second: bfloat16 [3, 640, 640], replicated, may hold values from -0.125 to 0.125
Outputs:
- edited: bfloat16 [16, 512, 640], P(('clips', 'frame'), 'row'), parts along dimension 0
There are 2 independent parts, one for each index of `clips`. A program takes and returns all parts, laid end to end along the dimension named above; an argument that names none is the same for every part. Nothing has to cross between parts.
Inputs may be any that keep to these rules, and one draw needn't show every extreme that they name: `key_index`: two different frame indices of the window, in either order; one of them is the window's last frame 8 - 1.
All inputs are finite; a program needn't handle non-finite values.
Results may differ from a plain program's by a relative error of at most 0.0067.
Values may be sent and summed in bfloat16 or wider, within the bound.
No kernel may reach another device: no remote copies, remote signals or barrier semaphores. Data moves between devices by JAX's collectives and lax.ppermute only.
A program may use at most 128 MiB of HBM per device.

v0:
```python
from functools import partial
import jax
import jax.numpy as jnp
from jax import lax
from jax.sharding import PartitionSpec as P

HEADS = 10
HEAD_DIM = 64


def from_root(value, axis, source):
    kept = jnp.where(lax.axis_index(axis) == source, value, 0).astype(value.dtype)
    return lax.psum(kept, axis)


def extended(array, sides, width):
    for axis, dim in sides:
        size, length = (lax.axis_size(axis), array.shape[dim])
        up = [(i, (i + 1) % size) for i in range(size - 1)]
        down = [(j, i) for i, j in up]
        last = lax.slice_in_dim(array, length - width, length, axis=dim)
        first = lax.slice_in_dim(array, 0, width, axis=dim)
        before = lax.ppermute(last, axis, up)
        after = lax.ppermute(first, axis, down)
        array = jnp.concatenate([before, array, after], axis=dim)
    return array


def temporal_mix(padded, weights, count):
    result = jnp.zeros((count * padded.shape[1], padded.shape[2]), jnp.float32)
    for offset in range(3):
        window = padded[offset : offset + count].reshape(-1, padded.shape[2])
        result = result + jnp.dot(window, weights[offset], preferred_element_type=jnp.float32)
    return result


def absorb_keys(query_heads, channels, state_now, kv_pieces, piece_start):
    highest, denominator, accumulated = state_now
    joined = jnp.concatenate(kv_pieces, axis=0)
    key_heads = joined[:, :channels].reshape(-1, HEADS, HEAD_DIM)
    value_heads = joined[:, channels:].reshape(-1, HEADS, HEAD_DIM)
    scores = jnp.einsum(
        "qhd,khd->hqk", query_heads, key_heads, preferred_element_type=jnp.float32
    ) * HEAD_DIM ** (-0.5)
    raised = jnp.maximum(highest, jnp.max(scores, axis=-1))
    kept_frac = jnp.exp(highest - raised)
    exponent = jnp.exp(scores - raised[:, :, None])
    denominator = jnp.sum(exponent, axis=-1)
    contrib = jnp.einsum(
        "hqk,khd->qhd",
        exponent.astype(jnp.bfloat16),
        value_heads,
        preferred_element_type=jnp.float32,
    )
    accumulated = accumulated * jnp.repeat(kept_frac.T, HEAD_DIM, axis=1) + contrib.reshape(
        contrib.shape[0], -1
    )
    return (raised, denominator, accumulated)


def shards(frames, key_index, w_query, w_keyval, w_out, norm_gain, w_first, w_second):
    frame_count, row_count, channels = frames.shape
    flattened = frames.reshape(-1, channels)
    queries = jnp.dot(flattened, w_query, preferred_element_type=jnp.float32).astype(jnp.bfloat16)
    query_heads = queries.reshape(-1, HEADS, HEAD_DIM)
    query_total = queries.shape[0]
    owners = key_index // frame_count
    chosen = frames[key_index % frame_count].reshape(-1, channels)
    keyval = jnp.dot(chosen, w_keyval, preferred_element_type=jnp.float32).astype(jnp.bfloat16)
    own_parts = (keyval[:row_count], keyval[row_count:])
    initial = (
        jnp.full((HEADS, query_total), -1e30, jnp.float32),
        jnp.zeros((HEADS, query_total), jnp.float32),
        jnp.zeros((query_total, channels), jnp.float32),
    )
    absorb = partial(absorb_keys, query_heads, channels)
    spread_parts = []
    for key_slot in range(2):
        spread_parts.append(from_root(own_parts[key_slot], "frame", owners[key_slot]))
    final = absorb(
        initial,
        (
            lax.all_gather(spread_parts[0], "row", axis=0, tiled=True),
            lax.all_gather(spread_parts[1], "row", axis=0, tiled=True),
        ),
        jnp.int32(0),
    )
    highest, denominator, accumulated = final
    mixed = accumulated.reshape(query_total, HEADS, HEAD_DIM) / denominator.T[:, :, None]
    attended = mixed.reshape(query_total, channels).astype(jnp.bfloat16)
    residual = flattened.astype(jnp.float32) + jnp.dot(
        attended, w_out, preferred_element_type=jnp.float32
    )
    mean_square = jnp.mean(residual * residual, axis=-1, keepdims=True)
    normed = (residual * lax.rsqrt(mean_square + 1e-06) * norm_gain).astype(jnp.bfloat16)
    normed = normed.reshape(frame_count, row_count, channels)
    padded = extended(normed, (("frame", 0),), 1)
    hidden = jax.nn.silu(temporal_mix(padded, w_first, frame_count)).astype(jnp.bfloat16)
    hidden = hidden.reshape(frame_count, row_count, channels)
    padded = extended(hidden, (("frame", 0),), 1)
    second = temporal_mix(padded, w_second, frame_count)
    return (residual + second).astype(jnp.bfloat16).reshape(frame_count, row_count, channels)


def solution(mesh):
    return jax.shard_map(
        shards,
        mesh=mesh,
        in_specs=(P(("clips", "frame"), "row", None), P("clips"), P(), P(), P(), P(), P(), P()),
        out_specs=P(("clips", "frame"), "row", None),
        check_vma=False,
    )
```

profile of v0, /device:TPU:1, one launch (start us, length us, event | category | flops | bytes accessed | tf_op | source)
XLA Modules:
  0.0 162.4 jit_solution(13678371207064377667)
XLA Ops:
  6.5 0.8 and_select_fusion.1
  9.2 1.6 gather_fusion
  10.8 0.7 convolution_convert_fusion
  11.5 0.9 slice_select_fusion
  12.5 34.7 %all-reduce.3.cloned.1.call-done = (bf16[128,1280]{1,0:T(8,128)(2,1)}, bf16[128,1280]{1,0:T(8,128)(2,1)}) async-done(((bf16[128,1280]{1,0:T(8,128)(2,1)}, bf16[128,1280]{1,0:T(8,128)(2,1)}), (bf16[128,1280]{1,0:T(8,128)(2,1)}, bf16[128,1280]{1,0:T(8,128)(2,1)})) %all-reduce.3.cloned.1.call-update) | async-done | bytes 655376 | tf_op jit(solution)/shard_map/psum | solution.py:13
  47.3 0.7 all-gather.5.cloned.1.call-update
  48.4 0.9 copy.12
  49.4 32.9 %all-gather.3.cloned.1.call-done = bf16[512,1280]{1,0:T(8,128)(2,1)} async-done(((bf16[128,1280]{1,0:T(8,128)(2,1)}), bf16[512,1280]{1,0:T(8,128)(2,1)}) %all-gather.3.cloned.1.call-update) | async-done | bytes 1310736 | tf_op jit(solution)/shard_map/all_gather | solution.py:83
  82.2 2.5 %constant_dynamic-update-slice_fusion.1 = bf16[1024,1280]{1,0:T(8,128)(2,1)} fusion(bf16[512,1280]{1,0:T(8,128)(2,1)} %all-gather.3.cloned.1.call-done), kind=kLoop, calls=%fused_computation.54 | loop fusion | bytes 2621440
  84.7 30.8 %all-gather.5.cloned.1.call-done = bf16[512,1280]{1,0:T(8,128)(2,1)} async-done(((bf16[128,1280]{1,0:T(8,128)(2,1)}), bf16[512,1280]{1,0:T(8,128)(2,1)}) %all-gather.5.cloned.1.call-update) | async-done | bytes 1310736 | tf_op jit(solution)/shard_map/all_gather | solution.py:84
  115.5 2.5 %constant_dynamic-update-slice_fusion = bf16[1024,1280]{1,0:T(8,128)(2,1)} fusion(bf16[1024,1280]{1,0:T(8,128)(2,1)} %constant_dynamic-update-slice_fusion.1, bf16[512,1280]{1,0:T(8,128)(2,1)} %all-gather.5.cloned.1.call-done), kind=kLoop, calls=%fused_computation.53 | loop fusion | bytes 2621440 | tf_op jit(solution)/shard_map/concatenate | solution.py:39
  118.0 3.5 %fusion.41 = (bf16[1024,640]{1,0:T(8,128)(2,1)}, bf16[1024,640]{1,0:T(8,128)(2,1)}) fusion(bf16[1024,1280]{1,0:T(8,128)(2,1)} %constant_dynamic-update-slice_fusion), kind=kLoop, calls=%fused_computation.63 | loop fusion | bytes 5242880 | tf_op jit(solution)/shard_map/slice | solution.py:40
  121.5 1.6 copy.13
  123.1 2.5 %copy.14 = bf16[1024,640]{0,1:T(8,128)(2,1)} copy(bf16[1024,640]{1,0:T(8,128)(2,1)} %get-tuple-element.8) | data formatting | bytes 2621440 | tf_op jit(solution)/shard_map/slice | solution.py:41
  125.5 2.6 %multiply_reduce_fusion = (f32[10,256]{1,0:T(8,128)S(1)}, f32[10,256,1024]{2,1,0:T(8,128)S(1)}) fusion(bf16[256,10,64]{0,2,1:T(8,128)(2,1)} %bitcast.74, bf16[1024,10,64]{0,2,1:T(8,128)(2,1)S(1)} %bitcast.69), kind=kOutput, calls=%fused_computation.2 | convolution fusion | flops 340784640 | bytes 12134400 | tf_op jit(solution)/shard_map/qhd,khd->hqk/dot_general | solution.py:42
  128.2 2.1 %fusion = f32[10,256]{1,0:T(8,128)S(1)} fusion(f32[10,256,1024]{2,1,0:T(8,128)S(1)} %get-tuple-element.26, f32[10,256]{1,0:T(8,128)S(1)} %get-tuple-element.20), kind=kLoop, calls=%fused_computation.3 | loop fusion | flops 7861760 | bytes 10506240 | tf_op jit(solution)/shard_map/reduce_sum | solution.py:48
  130.3 2.3 %fusion.19 = bf16[256,10,64]{0,2,1:T(8,128)(2,1)S(1)} fusion(bf16[1024,10,64]{0,2,1:T(8,128)(2,1)S(1)} %bitcast.77, f32[10,256,1024]{2,1,0:T(8,128)S(1)} %get-tuple-element.26, f32[10,256]{1,0:T(8,128)S(1)} %get-tuple-element.20, f32[256,10]{0,1:T(8,128)S(1)} %bitcast.82, f32[256,10]{0,1:T(8,128)S(1)} %get-tuple-element.19), kind=kOutput, calls=%fused_computation.20 | convolution fusion | flops 343900160 | bytes 12154880 | tf_op jit(solution)/shard_map/hqk,khd->qhd/dot_general | solution.py:49
  133.4 4.3 %collective-permute-start = (bf16[1,128,640]{2,1,0:T(8,128)(2,1)S(1)}, bf16[1,128,640]{2,1,0:T(8,128)(2,1)S(1)}, u32[]{:S(2)}, u32[]{:S(2)}) collective-permute-start(bf16[1,128,640]{2,1,0:T(8,128)(2,1)S(1)} %get-tuple-element.17), channel_id=1, source_target_pairs={{0,4},{4,8},{8,12},{1,5},{5,9},{9,13},{2,6},{6,10},{10,14},{3,7},{... | collective-permute-start | bytes 491528 | tf_op jit(solution)/shard_map/ppermute | solution.py:23
  137.7 1.9 %collective-permute-start.1 = (bf16[1,128,640]{2,1,0:T(8,128)(2,1)S(1)}, bf16[1,128,640]{2,1,0:T(8,128)(2,1)S(1)}, u32[]{:S(2)}, u32[]{:S(2)}) collective-permute-start(bf16[1,128,640]{2,1,0:T(8,128)(2,1)S(1)} %get-tuple-element.18), channel_id=1, source_target_pairs={{4,0},{8,4},{12,8},{5,1},{9,5},{13,9},{6,2},{10,6},{14,10},{7,3},{... | collective-permute-start | bytes 491528 | tf_op jit(solution)/shard_map/ppermute | solution.py:24
  140.1 4.2 %collective-permute-done.1 = bf16[1,128,640]{2,1,0:T(8,128)(2,1)S(1)} collective-permute-done((bf16[1,128,640]{2,1,0:T(8,128)(2,1)S(1)}, bf16[1,128,640]{2,1,0:T(8,128)(2,1)S(1)}, u32[]{:S(2)}, u32[]{:S(2)}) %collective-permute-start.1) | collective-permute-done | bytes 163872 | tf_op jit(solution)/shard_map/ppermute | solution.py:24
  145.4 2.1 %collective-permute-start.2 = (bf16[1,128,640]{2,1,0:T(8,128)(2,1)S(1)}, bf16[1,128,640]{2,1,0:T(8,128)(2,1)S(1)}, u32[]{:S(2)}, u32[]{:S(2)}) collective-permute-start(bf16[1,128,640]{2,1,0:T(8,128)(2,1)S(1)} %get-tuple-element.13), channel_id=1, source_target_pairs={{0,4},{4,8},{8,12},{1,5},{5,9},{9,13},{2,6},{6,10},{10,14},{3,7},{... | collective-permute-start | bytes 491528 | tf_op jit(solution)/shard_map/ppermute | solution.py:23
  147.5 2.4 %collective-permute-start.3 = (bf16[1,128,640]{2,1,0:T(8,128)(2,1)S(1)}, bf16[1,128,640]{2,1,0:T(8,128)(2,1)S(1)}, u32[]{:S(2)}, u32[]{:S(2)}) collective-permute-start(bf16[1,128,640]{2,1,0:T(8,128)(2,1)S(1)} %get-tuple-element.14), channel_id=1, source_target_pairs={{4,0},{8,4},{12,8},{5,1},{9,5},{13,9},{6,2},{10,6},{14,10},{7,3},{... | collective-permute-start | bytes 491528 | tf_op jit(solution)/shard_map/ppermute | solution.py:24
  150.4 3.7 %collective-permute-done.3 = bf16[1,128,640]{2,1,0:T(8,128)(2,1)S(1)} collective-permute-done((bf16[1,128,640]{2,1,0:T(8,128)(2,1)S(1)}, bf16[1,128,640]{2,1,0:T(8,128)(2,1)S(1)}, u32[]{:S(2)}, u32[]{:S(2)}) %collective-permute-start.3) | collective-permute-done | bytes 163872 | tf_op jit(solution)/shard_map/ppermute | solution.py:24
  154.7 1.2 fusion.15
  (39 shorter events, 4.5 us)
Async XLA Ops:
  6.5 4.3 %copy-start = (bf16[640,1280]{1,0:T(8,128)(2,1)S(1)}, bf16[640,1280]{1,0:T(8,128)(2,1)}, u32[]{:S(2)}) copy-start(bf16[640,1280]{1,0:T(8,128)(2,1)} %param.11) | copy-start | bytes 4915204
  6.5 40.7 %all-reduce.3.cloned.1.call-start = ((), (), s32[]{:S(2)}) async-start(), calls=%async_computation.2 | async-start | bytes 1310720 | tf_op jit(solution)/shard_map/psum | solution.py:13
  10.8 37.2 %copy-start.1 = (bf16[2,128,640]{2,1,0:T(8,128)(2,1)S(1)}, bf16[2,128,640]{2,1,0:T(8,128)(2,1)}, u32[]{:S(2)}) copy-start(bf16[2,128,640]{2,1,0:T(8,128)(2,1)} %param.8) | copy-start | bytes 983044
  10.8 37.2 %copy-start.5 = (bf16[640,640]{1,0:T(8,128)(2,1)S(1)}, bf16[640,640]{1,0:T(8,128)(2,1)}, u32[]{:S(2)}) copy-start(bf16[640,640]{1,0:T(8,128)(2,1)} %param.10) | copy-start | bytes 2457604
  12.5 69.8 %all-gather.3.cloned.1.call-start = ((), (), s32[]{:S(2)}) async-start(), calls=%async_computation | async-start | bytes 1638400 | tf_op jit(solution)/shard_map/all_gather | solution.py:83
  47.2 68.3 %all-gather.5.cloned.1.call-start = ((), (), s32[]{:S(2)}) async-start(), calls=%async_computation.1 | async-start | bytes 1638400 | tf_op jit(solution)/shard_map/all_gather | solution.py:84
  128.2 2.1 %copy-start.3 = (bf16[1024,640]{0,1:T(8,128)(2,1)S(1)}, bf16[1024,640]{0,1:T(8,128)(2,1)}, u32[]{:S(2)}) copy-start(bf16[1024,640]{0,1:T(8,128)(2,1)} %copy.14) | copy-start | bytes 3932164
  130.2 2.3 %copy-start.6 = (bf16[640,640]{1,0:T(8,128)(2,1)S(1)}, bf16[640,640]{1,0:T(8,128)(2,1)}, u32[]{:S(2)}) copy-start(bf16[640,640]{1,0:T(8,128)(2,1)} %param.12) | copy-start | bytes 2457604
  130.3 2.9 %copy-start.7 = (f32[640]{0:T(1024)S(1)}, f32[640]{0:T(1024)}, u32[]{:S(2)}) copy-start(f32[640]{0:T(1024)} %param.13) | copy-start | bytes 7684
  132.6 7.1 %copy-start.4 = (bf16[3,640,640]{2,1,0:T(8,128)(2,1)S(1)}, bf16[3,640,640]{2,1,0:T(8,128)(2,1)}, u32[]{:S(2)}) copy-start(bf16[3,640,640]{2,1,0:T(8,128)(2,1)} %param.14) | copy-start | bytes 7372804
  133.4 6.7 %collective-permute-start = (bf16[1,128,640]{2,1,0:T(8,128)(2,1)S(1)}, bf16[1,128,640]{2,1,0:T(8,128)(2,1)S(1)}, u32[]{:S(2)}, u32[]{:S(2)}) collective-permute-start(bf16[1,128,640]{2,1,0:T(8,128)(2,1)S(1)} %get-tuple-element.17), channel_id=1, source_target_pairs={{0,4},{4,8},{8,12},{1,5},{5,9},{9,13},{2,6},{6,10},{10,14},{3,7},{... | collective-permute-start | bytes 491528 | tf_op jit(solution)/shard_map/ppermute | solution.py:23
  137.7 6.6 %collective-permute-start.1 = (bf16[1,128,640]{2,1,0:T(8,128)(2,1)S(1)}, bf16[1,128,640]{2,1,0:T(8,128)(2,1)S(1)}, u32[]{:S(2)}, u32[]{:S(2)}) collective-permute-start(bf16[1,128,640]{2,1,0:T(8,128)(2,1)S(1)} %get-tuple-element.18), channel_id=1, source_target_pairs={{4,0},{8,4},{12,8},{5,1},{9,5},{13,9},{6,2},{10,6},{14,10},{7,3},{... | collective-permute-start | bytes 491528 | tf_op jit(solution)/shard_map/ppermute | solution.py:24
  144.9 5.1 %copy-start.2 = (bf16[3,640,640]{2,1,0:T(8,128)(2,1)S(1)}, bf16[3,640,640]{2,1,0:T(8,128)(2,1)}, u32[]{:S(2)}) copy-start(bf16[3,640,640]{2,1,0:T(8,128)(2,1)} %param.15) | copy-start | bytes 7372804
  145.4 5.0 %collective-permute-start.2 = (bf16[1,128,640]{2,1,0:T(8,128)(2,1)S(1)}, bf16[1,128,640]{2,1,0:T(8,128)(2,1)S(1)}, u32[]{:S(2)}, u32[]{:S(2)}) collective-permute-start(bf16[1,128,640]{2,1,0:T(8,128)(2,1)S(1)} %get-tuple-element.13), channel_id=1, source_target_pairs={{0,4},{4,8},{8,12},{1,5},{5,9},{9,13},{2,6},{6,10},{10,14},{3,7},{... | collective-permute-start | bytes 491528 | tf_op jit(solution)/shard_map/ppermute | solution.py:23
  147.5 6.6 %collective-permute-start.3 = (bf16[1,128,640]{2,1,0:T(8,128)(2,1)S(1)}, bf16[1,128,640]{2,1,0:T(8,128)(2,1)S(1)}, u32[]{:S(2)}, u32[]{:S(2)}) collective-permute-start(bf16[1,128,640]{2,1,0:T(8,128)(2,1)S(1)} %get-tuple-element.14), channel_id=1, source_target_pairs={{4,0},{8,4},{12,8},{5,1},{9,5},{13,9},{6,2},{10,6},{14,10},{7,3},{... | collective-permute-start | bytes 491528 | tf_op jit(solution)/shard_map/ppermute | solution.py:24
Sparse Core Ops, SparseCore 0:
  12.6 34.5 all-reduce.2
  48.8 33.4 all-gather.2
  83.8 31.6 all-gather.4
where the time goes:
time: 163 us; the launch traced here: 162 us
  waiting for transfers between devices  107 us (66%)
  local copies, waits for them, and re-layouts  15.6 us (10%)
  between operations  14.7 us (9%)
  starting transfers between devices  10.8 us (7%)
  matrix products  10.2 us (6%)
  other arithmetic  4.05 us (2%)
    psum x1, waiting for transfers between devices, from_root(): return lax.psum(kept, axis)  34.7 us
    all_gather x1, waiting for transfers between devices, shards(): lax.all_gather(spread_parts[0], 'row', axis=0, tiled=True)  32.9 us
    all_gather x1, waiting for transfers between devices, shards(): lax.all_gather(spread_parts[1], 'row', axis=0, tiled=True)  30.8 us
    ppermute x2, waiting for transfers between devices, extended(): after = lax.ppermute(first, axis, down)  7.96 us
    ppermute x2, starting transfers between devices, extended(): before = lax.ppermute(last, axis, up)  6.37 us
    slice x2, local copies, waits for them, and re-layouts, absorb_keys(): key_heads = joined[:, :channels].reshape(-1, HEADS, HEAD_DIM)  5.06 us
    ppermute x2, starting transfers between devices, extended(): after = lax.ppermute(first, axis, down)  4.33 us
    dot_general x6, matrix products, temporal_mix(): jnp.dot(window, weights[offset], preferred_element_type=jnp.float32)  3.53 us
  transfers between devices with their start and end apart: 7, of which 5 were waited for; matrix products, arithmetic and copies ran while one was open for 3% of the time, Pallas kernels for 0%

commit v1 on v0

--- a/solution.py
+++ b/solution.py
@@ -10,7 +10,7 @@
 
 def from_root(value, axis, source):
     kept = jnp.where(lax.axis_index(axis) == source, value, 0).astype(value.dtype)
-    return lax.psum(kept, axis)
+    return jnp.sum(lax.all_gather(kept, axis), axis=0)
 
 
 def extended(array, sides, width):

time: 163 us -> 167 us (1.025)
  other arithmetic: 4.05 us -> 8.68 us
    all_gather x0 -> x2, waiting for transfers between devices: none -> 37.4 us  [from_root(): return jnp.sum(lax.all_gather(kept, axis), axis=0)]
    psum x1 -> x0, waiting for transfers between devices: 34.7 us -> none  [from_root(): return lax.psum(kept, axis)]
    reduce_sum x0 -> x2, other arithmetic: none -> 4.64 us  [from_root(): return jnp.sum(lax.all_gather(kept, axis), axis=0)]
    all_gather x1, waiting for transfers between devices: 32.9 us -> 29.5 us  [shards(): lax.all_gather(spread_parts[0], 'row', axis=0, tiled=True)]
  transfers between devices with their start and end apart: 7 -> 8, of which waited for: 5 -> 6; matrix products, arithmetic and copies ran while one was open for 3% -> 6% of each run, Pallas kernels for 0% -> 0%
where the time goes in v1:
time: 167 us; the launch traced here: 166 us
  waiting for transfers between devices  106 us (63%)
  local copies, waits for them, and re-layouts  15.7 us (9%)
  between operations  14.6 us (9%)
  starting transfers between devices  10.8 us (6%)
  matrix products  10.2 us (6%)
  other arithmetic  8.68 us (5%)
    all_gather x2, waiting for transfers between devices, from_root(): return jnp.sum(lax.all_gather(kept, axis), axis=0)  37.4 us
    all_gather x1, waiting for transfers between devices, shards(): lax.all_gather(spread_parts[1], 'row', axis=0, tiled=True)  30.7 us
    all_gather x1, waiting for transfers between devices, shards(): lax.all_gather(spread_parts[0], 'row', axis=0, tiled=True)  29.5 us
    ppermute x2, waiting for transfers between devices, extended(): after = lax.ppermute(first, axis, down)  7.96 us
    ppermute x2, starting transfers between devices, extended(): before = lax.ppermute(last, axis, up)  6.37 us
    slice x2, local copies, waits for them, and re-layouts, absorb_keys(): key_heads = joined[:, :channels].reshape(-1, HEADS, HEAD_DIM)  5.06 us
    reduce_sum x2, other arithmetic, from_root(): return jnp.sum(lax.all_gather(kept, axis), axis=0)  4.64 us
    ppermute x2, starting transfers between devices, extended(): after = lax.ppermute(first, axis, down)  4.33 us
  transfers between devices with their start and end apart: 8, of which 6 were waited for; matrix products, arithmetic and copies ran while one was open for 6% of the time, Pallas kernels for 0%

profile of v1, /device:TPU:1, one launch (start us, length us, event | category | flops | bytes accessed | tf_op | source)
XLA Modules:
  0.0 166.3 jit_solution(2893601016496983775)
XLA Ops:
  9.1 1.6 gather_fusion
  11.4 0.9 slice_select_fusion
  13.1 20.0 %all-gather.11.cloned.1.call-done = bf16[512,1280]{1,0:T(8,128)(2,1)} async-done(((bf16[128,1280]{1,0:T(8,128)(2,1)}), bf16[512,1280]{1,0:T(8,128)(2,1)}) %all-gather.11.cloned.1.call-update) | async-done | bytes 1310736 | tf_op jit(solution)/shard_map/all_gather | solution.py:13
  33.2 2.3 %reduce_sum.42 = bf16[128,1280]{1,0:T(8,128)(2,1)} reduce(bf16[4,128,1280]{2,1,0:T(8,128)(2,1)} %bitcast.80, bf16[]{:T(256)} %constant.48.clone.1), dimensions={0}, to_apply=%region_0.1 | reduce | flops 491520 | bytes 1638402 | tf_op jit(solution)/shard_map/reduce_sum | solution.py:13
  35.6 17.4 %all-gather.13.cloned.1.call-done = bf16[512,1280]{1,0:T(8,128)(2,1)} async-done(((bf16[128,1280]{1,0:T(8,128)(2,1)}), bf16[512,1280]{1,0:T(8,128)(2,1)}) %all-gather.13.cloned.1.call-update) | async-done | bytes 1310736 | tf_op jit(solution)/shard_map/all_gather | solution.py:13
  53.0 2.3 %reduce_sum.43 = bf16[128,1280]{1,0:T(8,128)(2,1)} reduce(bf16[4,128,1280]{2,1,0:T(8,128)(2,1)} %bitcast.79, bf16[]{:T(256)} %constant.48.clone.1), dimensions={0}, to_apply=%region_1.2 | reduce | flops 491520 | bytes 1638402 | tf_op jit(solution)/shard_map/reduce_sum | solution.py:13
  55.8 0.9 copy.11
  56.7 29.5 %all-gather.7.cloned.1.call-done = bf16[512,1280]{1,0:T(8,128)(2,1)} async-done(((bf16[128,1280]{1,0:T(8,128)(2,1)}), bf16[512,1280]{1,0:T(8,128)(2,1)}) %all-gather.7.cloned.1.call-update) | async-done | bytes 1310736 | tf_op jit(solution)/shard_map/all_gather | solution.py:83
  86.2 2.5 %constant_dynamic-update-slice_fusion.1 = bf16[1024,1280]{1,0:T(8,128)(2,1)} fusion(bf16[512,1280]{1,0:T(8,128)(2,1)} %all-gather.7.cloned.1.call-done), kind=kLoop, calls=%fused_computation.54 | loop fusion | bytes 2621440
  88.7 30.7 %all-gather.9.cloned.1.call-done = bf16[512,1280]{1,0:T(8,128)(2,1)} async-done(((bf16[128,1280]{1,0:T(8,128)(2,1)}), bf16[512,1280]{1,0:T(8,128)(2,1)}) %all-gather.9.cloned.1.call-update) | async-done | bytes 1310736 | tf_op jit(solution)/shard_map/all_gather | solution.py:84
  119.4 2.5 %constant_dynamic-update-slice_fusion = bf16[1024,1280]{1,0:T(8,128)(2,1)} fusion(bf16[1024,1280]{1,0:T(8,128)(2,1)} %constant_dynamic-update-slice_fusion.1, bf16[512,1280]{1,0:T(8,128)(2,1)} %all-gather.9.cloned.1.call-done), kind=kLoop, calls=%fused_computation.53 | loop fusion | bytes 2621440 | tf_op jit(solution)/shard_map/concatenate | solution.py:39
  121.8 3.5 %fusion.41 = (bf16[1024,640]{1,0:T(8,128)(2,1)}, bf16[1024,640]{1,0:T(8,128)(2,1)}) fusion(bf16[1024,1280]{1,0:T(8,128)(2,1)} %constant_dynamic-update-slice_fusion), kind=kLoop, calls=%fused_computation.63 | loop fusion | bytes 5242880 | tf_op jit(solution)/shard_map/slice | solution.py:40
  125.3 1.6 copy.12
  126.9 2.5 %copy.13 = bf16[1024,640]{0,1:T(8,128)(2,1)} copy(bf16[1024,640]{1,0:T(8,128)(2,1)} %get-tuple-element.6) | data formatting | bytes 2621440 | tf_op jit(solution)/shard_map/slice | solution.py:41
  129.4 2.6 %multiply_reduce_fusion = (f32[10,256]{1,0:T(8,128)S(1)}, f32[10,256,1024]{2,1,0:T(8,128)S(1)}) fusion(bf16[256,10,64]{0,2,1:T(8,128)(2,1)} %bitcast.76, bf16[1024,10,64]{0,2,1:T(8,128)(2,1)S(1)} %bitcast.71), kind=kOutput, calls=%fused_computation.2 | convolution fusion | flops 340784640 | bytes 12134400 | tf_op jit(solution)/shard_map/qhd,khd->hqk/dot_general | solution.py:42
  132.0 2.1 %fusion = f32[10,256]{1,0:T(8,128)S(1)} fusion(f32[10,256,1024]{2,1,0:T(8,128)S(1)} %get-tuple-element.24, f32[10,256]{1,0:T(8,128)S(1)} %get-tuple-element.18), kind=kLoop, calls=%fused_computation.3 | loop fusion | flops 7861760 | bytes 10506240 | tf_op jit(solution)/shard_map/reduce_sum | solution.py:48
  134.1 2.3 %fusion.19 = bf16[256,10,64]{0,2,1:T(8,128)(2,1)S(1)} fusion(bf16[1024,10,64]{0,2,1:T(8,128)(2,1)S(1)} %bitcast.81, f32[10,256,1024]{2,1,0:T(8,128)S(1)} %get-tuple-element.24, f32[10,256]{1,0:T(8,128)S(1)} %get-tuple-element.18, f32[256,10]{0,1:T(8,128)S(1)} %bitcast.86, f32[256,10]{0,1:T(8,128)S(1)} %get-tuple-element.17), kind=kOutput, calls=%fused_computation.20 | convolution fusion | flops 343900160 | bytes 12154880 | tf_op jit(solution)/shard_map/hqk,khd->qhd/dot_general | solution.py:49
  137.2 4.3 %collective-permute-start = (bf16[1,128,640]{2,1,0:T(8,128)(2,1)S(1)}, bf16[1,128,640]{2,1,0:T(8,128)(2,1)S(1)}, u32[]{:S(2)}, u32[]{:S(2)}) collective-permute-start(bf16[1,128,640]{2,1,0:T(8,128)(2,1)S(1)} %get-tuple-element.15), channel_id=1, source_target_pairs={{0,4},{4,8},{8,12},{1,5},{5,9},{9,13},{2,6},{6,10},{10,14},{3,7},{... | collective-permute-start | bytes 491528 | tf_op jit(solution)/shard_map/ppermute | solution.py:23
  141.6 1.9 %collective-permute-start.1 = (bf16[1,128,640]{2,1,0:T(8,128)(2,1)S(1)}, bf16[1,128,640]{2,1,0:T(8,128)(2,1)S(1)}, u32[]{:S(2)}, u32[]{:S(2)}) collective-permute-start(bf16[1,128,640]{2,1,0:T(8,128)(2,1)S(1)} %get-tuple-element.16), channel_id=1, source_target_pairs={{4,0},{8,4},{12,8},{5,1},{9,5},{13,9},{6,2},{10,6},{14,10},{7,3},{... | collective-permute-start | bytes 491528 | tf_op jit(solution)/shard_map/ppermute | solution.py:24
  144.0 4.2 %collective-permute-done.1 = bf16[1,128,640]{2,1,0:T(8,128)(2,1)S(1)} collective-permute-done((bf16[1,128,640]{2,1,0:T(8,128)(2,1)S(1)}, bf16[1,128,640]{2,1,0:T(8,128)(2,1)S(1)}, u32[]{:S(2)}, u32[]{:S(2)}) %collective-permute-start.1) | collective-permute-done | bytes 163872 | tf_op jit(solution)/shard_map/ppermute | solution.py:24
  149.3 2.1 %collective-permute-start.2 = (bf16[1,128,640]{2,1,0:T(8,128)(2,1)S(1)}, bf16[1,128,640]{2,1,0:T(8,128)(2,1)S(1)}, u32[]{:S(2)}, u32[]{:S(2)}) collective-permute-start(bf16[1,128,640]{2,1,0:T(8,128)(2,1)S(1)} %get-tuple-element.11), channel_id=1, source_target_pairs={{0,4},{4,8},{8,12},{1,5},{5,9},{9,13},{2,6},{6,10},{10,14},{3,7},{... | collective-permute-start | bytes 491528 | tf_op jit(solution)/shard_map/ppermute | solution.py:23
  151.4 2.4 %collective-permute-start.3 = (bf16[1,128,640]{2,1,0:T(8,128)(2,1)S(1)}, bf16[1,128,640]{2,1,0:T(8,128)(2,1)S(1)}, u32[]{:S(2)}, u32[]{:S(2)}) collective-permute-start(bf16[1,128,640]{2,1,0:T(8,128)(2,1)S(1)} %get-tuple-element.12), channel_id=1, source_target_pairs={{4,0},{8,4},{12,8},{5,1},{9,5},{13,9},{6,2},{10,6},{14,10},{7,3},{... | collective-permute-start | bytes 491528 | tf_op jit(solution)/shard_map/ppermute | solution.py:24
  154.3 3.7 %collective-permute-done.3 = bf16[1,128,640]{2,1,0:T(8,128)(2,1)S(1)} collective-permute-done((bf16[1,128,640]{2,1,0:T(8,128)(2,1)S(1)}, bf16[1,128,640]{2,1,0:T(8,128)(2,1)S(1)}, u32[]{:S(2)}, u32[]{:S(2)}) %collective-permute-start.3) | collective-permute-done | bytes 163872 | tf_op jit(solution)/shard_map/ppermute | solution.py:24
  158.5 1.2 fusion.15
  (44 shorter events, 6.7 us)
Async XLA Ops:
  6.5 4.2 %copy-start = (bf16[640,1280]{1,0:T(8,128)(2,1)S(1)}, bf16[640,1280]{1,0:T(8,128)(2,1)}, u32[]{:S(2)}) copy-start(bf16[640,1280]{1,0:T(8,128)(2,1)} %param.11) | copy-start | bytes 4915204
  6.5 26.6 %all-gather.11.cloned.1.call-start = ((), (), s32[]{:S(2)}) async-start(), calls=%async_computation.2 | async-start | bytes 1638400 | tf_op jit(solution)/shard_map/all_gather | solution.py:13
  12.3 43.0 %copy-start.1 = (bf16[2,128,640]{2,1,0:T(8,128)(2,1)S(1)}, bf16[2,128,640]{2,1,0:T(8,128)(2,1)}, u32[]{:S(2)}) copy-start(bf16[2,128,640]{2,1,0:T(8,128)(2,1)} %param.8) | copy-start | bytes 983044
  12.3 43.0 %copy-start.5 = (bf16[640,640]{1,0:T(8,128)(2,1)S(1)}, bf16[640,640]{1,0:T(8,128)(2,1)}, u32[]{:S(2)}) copy-start(bf16[640,640]{1,0:T(8,128)(2,1)} %param.10) | copy-start | bytes 2457604
  12.4 40.6 %all-gather.13.cloned.1.call-start = ((), (), s32[]{:S(2)}) async-start(), calls=%async_computation.3 | async-start | bytes 1638400 | tf_op jit(solution)/shard_map/all_gather | solution.py:13
  13.1 73.1 %all-gather.7.cloned.1.call-start = ((), (), s32[]{:S(2)}) async-start(), calls=%async_computation | async-start | bytes 1638400 | tf_op jit(solution)/shard_map/all_gather | solution.py:83
  35.5 83.8 %all-gather.9.cloned.1.call-start = ((), (), s32[]{:S(2)}) async-start(), calls=%async_computation.1 | async-start | bytes 1638400 | tf_op jit(solution)/shard_map/all_gather | solution.py:84
  132.0 2.1 %copy-start.3 = (bf16[1024,640]{0,1:T(8,128)(2,1)S(1)}, bf16[1024,640]{0,1:T(8,128)(2,1)}, u32[]{:S(2)}) copy-start(bf16[1024,640]{0,1:T(8,128)(2,1)} %copy.13) | copy-start | bytes 3932164
  134.1 2.3 %copy-start.6 = (bf16[640,640]{1,0:T(8,128)(2,1)S(1)}, bf16[640,640]{1,0:T(8,128)(2,1)}, u32[]{:S(2)}) copy-start(bf16[640,640]{1,0:T(8,128)(2,1)} %param.12) | copy-start | bytes 2457604
  134.1 2.9 %copy-start.7 = (f32[640]{0:T(1024)S(1)}, f32[640]{0:T(1024)}, u32[]{:S(2)}) copy-start(f32[640]{0:T(1024)} %param.13) | copy-start | bytes 7684
  136.4 7.1 %copy-start.4 = (bf16[3,640,640]{2,1,0:T(8,128)(2,1)S(1)}, bf16[3,640,640]{2,1,0:T(8,128)(2,1)}, u32[]{:S(2)}) copy-start(bf16[3,640,640]{2,1,0:T(8,128)(2,1)} %param.14) | copy-start | bytes 7372804
  137.2 6.7 %collective-permute-start = (bf16[1,128,640]{2,1,0:T(8,128)(2,1)S(1)}, bf16[1,128,640]{2,1,0:T(8,128)(2,1)S(1)}, u32[]{:S(2)}, u32[]{:S(2)}) collective-permute-start(bf16[1,128,640]{2,1,0:T(8,128)(2,1)S(1)} %get-tuple-element.15), channel_id=1, source_target_pairs={{0,4},{4,8},{8,12},{1,5},{5,9},{9,13},{2,6},{6,10},{10,14},{3,7},{... | collective-permute-start | bytes 491528 | tf_op jit(solution)/shard_map/ppermute | solution.py:23
  141.6 6.6 %collective-permute-start.1 = (bf16[1,128,640]{2,1,0:T(8,128)(2,1)S(1)}, bf16[1,128,640]{2,1,0:T(8,128)(2,1)S(1)}, u32[]{:S(2)}, u32[]{:S(2)}) collective-permute-start(bf16[1,128,640]{2,1,0:T(8,128)(2,1)S(1)} %get-tuple-element.16), channel_id=1, source_target_pairs={{4,0},{8,4},{12,8},{5,1},{9,5},{13,9},{6,2},{10,6},{14,10},{7,3},{... | collective-permute-start | bytes 491528 | tf_op jit(solution)/shard_map/ppermute | solution.py:24
  148.7 5.1 %copy-start.2 = (bf16[3,640,640]{2,1,0:T(8,128)(2,1)S(1)}, bf16[3,640,640]{2,1,0:T(8,128)(2,1)}, u32[]{:S(2)}) copy-start(bf16[3,640,640]{2,1,0:T(8,128)(2,1)} %param.15) | copy-start | bytes 7372804
  149.3 5.0 %collective-permute-start.2 = (bf16[1,128,640]{2,1,0:T(8,128)(2,1)S(1)}, bf16[1,128,640]{2,1,0:T(8,128)(2,1)S(1)}, u32[]{:S(2)}, u32[]{:S(2)}) collective-permute-start(bf16[1,128,640]{2,1,0:T(8,128)(2,1)S(1)} %get-tuple-element.11), channel_id=1, source_target_pairs={{0,4},{4,8},{8,12},{1,5},{5,9},{9,13},{2,6},{6,10},{10,14},{3,7},{... | collective-permute-start | bytes 491528 | tf_op jit(solution)/shard_map/ppermute | solution.py:23
  151.4 6.6 %collective-permute-start.3 = (bf16[1,128,640]{2,1,0:T(8,128)(2,1)S(1)}, bf16[1,128,640]{2,1,0:T(8,128)(2,1)S(1)}, u32[]{:S(2)}, u32[]{:S(2)}) collective-permute-start(bf16[1,128,640]{2,1,0:T(8,128)(2,1)S(1)} %get-tuple-element.12), channel_id=1, source_target_pairs={{4,0},{8,4},{12,8},{5,1},{9,5},{13,9},{6,2},{10,6},{14,10},{7,3},{... | collective-permute-start | bytes 491528 | tf_op jit(solution)/shard_map/ppermute | solution.py:24
Sparse Core Ops, SparseCore 0:
  12.5 20.6 all-gather.10
  34.7 18.1 all-gather.12
  54.5 31.6 all-gather.6
  87.6 31.6 all-gather.8
